TPU v7x, 512 devices: a whole 4x8x8 slice. The times are simulated.
512 devices in a mesh: dom: 32 (over x, z), strip: 16 (over y, core).
Axes of the slice: x: 4, y: 8, z: 8, core: 2. Of those that a mesh axis runs over, the one named last changes fastest.
Arguments:
- state: float32 [32, 4, 512, 512], P('dom', None, 'strip'), may hold values from -6 to 6
- copies: int32 [32], replicated, may hold values from 0 to 31
- depth: float32 [512, 512], P('strip'), may hold values from 0.5 to 2
- friction: float32 [512, 512], P('strip'), may hold values from 0.05 to 0.5
- obs_cells: int32 [16, 512], P('strip'), may hold values from 0 to 16383
- obs_values: float32 [16, 512], P('strip'), may hold values from -6 to 6
Outputs:
- forecast: float32 [32, 4, 512, 512], P('dom', None, 'strip')
- log_weights: float32 [32], P('dom')
All inputs are finite; a program needn't handle non-finite values.
Results may differ from a plain program's by a relative error of at most 0.000039.
Values sent between devices are 32-bit elements; how exact they have to be, the bound alone decides.
No kernel may reach another device: no remote copies, remote signals or barrier semaphores. Data moves between devices by JAX's collectives and lax.ppermute only.
A program may use at most 64 MiB of HBM per device.

v0:
```python
import jax
import jax.numpy as jnp
from jax import lax
from jax.sharding import PartitionSpec as P

STEPS = 4
time_step = 0.25
coriolis = 0.3
diffusion = 0.2
obs_variance = 4.0


def padded_2(cells, sides, width):
    for axis, dim in sides:
        count = lax.axis_size(axis)
        ends = count - 1
        head = lax.slice_in_dim(cells, 0, width, axis=dim)
        tail = lax.slice_in_dim(cells, cells.shape[dim] - width, cells.shape[dim], axis=dim)
        cells = jnp.concatenate(
            [
                lax.ppermute(tail, axis, [(i, (i + 1) % count) for i in range(ends)]),
                cells,
                lax.ppermute(head, axis, [((i + 1) % count, i) for i in range(ends)]),
            ],
            axis=dim,
        )
    return cells


def diff_cols(a):
    return (jnp.roll(a, -1, axis=-1) - jnp.roll(a, 1, axis=-1)) * 0.5


def advance(padded, deep, drag, valid):
    eta, velo_u, velo_v, tracer = (padded[:, 0], padded[:, 1], padded[:, 2], padded[:, 3])
    flux_x = deep * velo_u
    flux_y = deep * velo_v
    eta_ext = eta[:, 1:-1] - time_step * (
        diff_cols(flux_x)[:, 1:-1] + (flux_y[:, 2:] - flux_y[:, :-2]) * 0.5
    )
    eta_ext = jnp.where(valid, eta_ext, 0.0)
    eta_new = eta_ext[:, 1:-1]
    inner_u = velo_u[:, 2:-2]
    inner_v = velo_v[:, 2:-2]
    inner_r = drag[2:-2]
    u_new = (
        inner_u
        - time_step * diff_cols(eta_new)
        - time_step * inner_r * inner_u
        + time_step * coriolis * inner_v
    )
    v_new = (
        inner_v
        - time_step * ((eta_ext[:, 2:] - eta_ext[:, :-2]) * 0.5)
        - time_step * inner_r * inner_v
        - time_step * coriolis * inner_u
    )
    inner_c = tracer[:, 2:-2]
    upper = tracer[:, 3:-1]
    lower = tracer[:, 1:-3]
    grad_y = (upper - lower) * 0.5
    laplace = (
        upper
        + lower
        + jnp.roll(inner_c, -1, axis=-1)
        + jnp.roll(inner_c, 1, axis=-1)
        - 4.0 * inner_c
    )
    c_new = (
        inner_c
        - time_step * (inner_u * diff_cols(inner_c) + inner_v * grad_y)
        + time_step * diffusion * laplace
    )
    return jnp.stack([eta_new, u_new, v_new, c_new], axis=1)


def local(state, copies, depth, friction, obs_cells, obs_values):
    per_dev = state.shape[0]
    rows = state.shape[2]
    member_idx = lax.axis_index("dom")
    sources = lax.dynamic_slice_in_dim(copies, member_idx * per_dev, per_dev, 0)
    piece = lax.all_gather(state, "dom", axis=0, tiled=True)
    labels = jnp.arange(piece.shape[0], dtype=jnp.int32)
    hit = labels == sources[0]
    picks = [jnp.sum(jnp.where(hit[:, None, None, None], piece, 0.0), axis=0)]
    member = jnp.stack(picks)
    margin = 2 * STEPS
    statics = padded_2(jnp.stack([depth, friction]), (("strip", 1),), margin)
    strip_idx = lax.axis_index("strip")
    row_all = strip_idx * rows - margin + jnp.arange(rows + 2 * margin, dtype=jnp.int32)
    inside_all = ((row_all >= 0) & (row_all < rows * lax.axis_size("strip")))[:, None]
    for step in range(STEPS):
        padded = padded_2(member, (("strip", 2),), 2)
        offset = margin - 2
        span = rows + 2 * 2
        deep = statics[0, offset : offset + span]
        drag = statics[1, offset : offset + span]
        valid = inside_all[offset + 1 : offset + span - 1]
        kept = inside_all[offset + 2 : offset + span - 2]
        result = advance(padded, deep, drag, valid)
        member = jnp.where(kept[None, None], result, 0.0)
    eta = member[:, 0].reshape(per_dev, -1)
    seen = jnp.take(eta, obs_cells[0], axis=1)
    gap = seen - obs_values[0][None, :]
    partial_value = -jnp.sum(gap * gap, axis=1) * (0.5 / obs_variance)
    summed = lax.psum(partial_value, "strip")
    loglik = lax.all_gather(summed, "dom", axis=0, tiled=True)
    top = jnp.max(loglik)
    total = top + jnp.log(jnp.sum(jnp.exp(loglik - top)))
    mine = lax.dynamic_slice_in_dim(loglik - total, member_idx * per_dev, per_dev, 0)
    return (member, mine)


def solution(mesh):
    placed = (
        P("dom", None, "strip", None),
        P(),
        P("strip", None),
        P("strip", None),
        P("strip", None),
        P("strip", None),
    )
    return jax.shard_map(
        local,
        mesh=mesh,
        in_specs=placed,
        out_specs=(P("dom", None, "strip", None), P("dom")),
        check_vma=False,
    )
```

profile of v0, /device:TPU:32, one launch (start us, length us, event | category | flops | bytes accessed | tf_op | source)
XLA Modules:
  0.0 276.5 jit_solution(14515473599032346318)
XLA Ops:
  7.2 0.7 all-gather.2.cloned.1.call-update
  7.9 0.8 pad_maximum_fusion.24
  8.7 1.9 collective-permute-start.2
  10.6 4.9 %collective-permute-start.3 = (f32[2,8,512]{2,1,0:T(8,128)S(1)}, f32[2,8,512]{2,1,0:T(8,128)S(1)}, u32[]{:S(2)}, u32[]{:S(2)}) collective-permute-start(f32[2,8,512]{2,1,0:T(8,128)S(1)} %get-tuple-element.43), channel_id=1, source_target_pairs={{1,0},{2,1},{3,2},{4,3},{5,4},{6,5},{7,6},{8,7},{9,8},{10,9},{11,1... | collective-permute-start | bytes 98312 | tf_op jit(solution)/shard_map/ppermute | solution.py:23
  15.5 1.2 dynamic_slice.6
  16.7 0.6 iota_compare_fusion
  17.4 102.1 %all-gather.2.cloned.1.call-done = f32[32,4,32,512]{3,2,1,0:T(8,128)} async-done(((f32[1,4,32,512]{3,2,1,0:T(8,128)}), f32[32,4,32,512]{3,2,1,0:T(8,128)}) %all-gather.2.cloned.1.call-update) | async-done | bytes 8388624 | tf_op jit(solution)/shard_map/all_gather | solution.py:82
  119.5 4.6 %select_reduce_fusion = f32[4,32,512]{2,1,0:T(8,128)S(1)} fusion(f32[32,4,32,512]{3,2,1,0:T(8,128)} %all-gather.2.cloned.1.call-done, pred[32]{0:T(512)(128)(4,1)S(1)} %iota_compare_fusion), kind=kLoop, calls=%fused_computation.1 | loop fusion | flops 4128768 | bytes 8650784 | tf_op jit(solution)/shard_map/reduce_sum | solution.py:85
  124.2 1.9 collective-permute-start
  126.1 4.9 %collective-permute-start.1 = (f32[1,4,2,512]{3,2,1,0:T(2,128)S(1)}, f32[1,4,2,512]{3,2,1,0:T(2,128)S(1)}, u32[]{:S(2)}, u32[]{:S(2)}) collective-permute-start(f32[1,4,2,512]{3,2,1,0:T(2,128)S(1)} %get-tuple-element.33), channel_id=1, source_target_pairs={{1,0},{2,1},{3,2},{4,3},{5,4},{6,5},{7,6},{8,7},{9,8},{10,9},{11,1... | collective-permute-start | bytes 49160 | tf_op jit(solution)/shard_map/ppermute | solution.py:23
  131.1 1.3 collective-permute-done.1
  132.7 0.1 fusion.25
  132.8 0.1 fusion.100
  133.1 0.1 fusion.52
  133.2 0.1 add_bitcast_fusion.3
  133.4 0.1 maximum_select_fusion
  133.5 1.9 collective-permute-start.4
  135.4 4.9 %collective-permute-start.5 = (f32[1,4,2,512]{3,2,1,0:T(2,128)S(1)}, f32[1,4,2,512]{3,2,1,0:T(2,128)S(1)}, u32[]{:S(2)}, u32[]{:S(2)}) collective-permute-start(f32[1,4,2,512]{3,2,1,0:T(2,128)S(1)} %get-tuple-element.31), channel_id=1, source_target_pairs={{1,0},{2,1},{3,2},{4,3},{5,4},{6,5},{7,6},{8,7},{9,8},{10,9},{11,1... | collective-permute-start | bytes 49160 | tf_op jit(solution)/shard_map/ppermute | solution.py:23
  140.3 1.4 collective-permute-done.5
  142.0 0.1 fusion.18
  142.1 0.1 fusion.94
  142.4 0.1 fusion.57
  142.5 0.1 add_bitcast_fusion.2
  142.6 0.1 maximum_select_fusion.1
  142.7 1.9 collective-permute-start.6
  144.7 4.9 %collective-permute-start.7 = (f32[1,4,2,512]{3,2,1,0:T(2,128)S(1)}, f32[1,4,2,512]{3,2,1,0:T(2,128)S(1)}, u32[]{:S(2)}, u32[]{:S(2)}) collective-permute-start(f32[1,4,2,512]{3,2,1,0:T(2,128)S(1)} %get-tuple-element.29), channel_id=1, source_target_pairs={{1,0},{2,1},{3,2},{4,3},{5,4},{6,5},{7,6},{8,7},{9,8},{10,9},{11,1... | collective-permute-start | bytes 49160 | tf_op jit(solution)/shard_map/ppermute | solution.py:23
  149.5 1.4 collective-permute-done.7
  151.2 0.1 fusion.11
  151.3 0.1 fusion.88
  151.6 0.1 fusion.62
  151.8 0.1 add_bitcast_fusion.1
  151.9 0.1 maximum_select_fusion.2
  152.0 1.9 collective-permute-start.8
  153.9 4.9 %collective-permute-start.9 = (f32[1,4,2,512]{3,2,1,0:T(2,128)S(1)}, f32[1,4,2,512]{3,2,1,0:T(2,128)S(1)}, u32[]{:S(2)}, u32[]{:S(2)}) collective-permute-start(f32[1,4,2,512]{3,2,1,0:T(2,128)S(1)} %get-tuple-element.27), channel_id=1, source_target_pairs={{1,0},{2,1},{3,2},{4,3},{5,4},{6,5},{7,6},{8,7},{9,8},{10,9},{11,1... | collective-permute-start | bytes 49160 | tf_op jit(solution)/shard_map/ppermute | solution.py:23
  158.8 1.3 dynamic-slice
  160.1 0.1 collective-permute-done.9
  160.5 0.1 fusion.4
  160.9 0.1 fusion.67
  161.0 0.1 add_bitcast_fusion
  161.1 0.1 maximum_select_fusion.3
  161.3 3.1 %gather_fusion = f32[512]{0:T(512)S(1)} fusion(f32[16384]{0:T(1024)S(1)} %bitcast.118, s32[1024]{0:T(1024)S(1)} %pad_clamp_fusion), kind=kCustom, calls=%fused_computation | custom fusion | bytes 6144 | tf_op jit(solution)/shard_map/jit(_take)/gather | solution.py:103
  164.4 0.6 multiply_reduce_fusion
  165.7 27.6 %psum.7 = f32[1]{0:T(128)} all-reduce(f32[1]{0:T(128)} %bitcast.40), channel_id=1, replica_groups=mesh['dom'=32,'strip'=16] {'strip'}, use_global_device_ids=true, to_apply=%region_2.3 | all-reduce | flops 1 | bytes 8 | tf_op jit(solution)/shard_map/psum | solution.py:106
  193.3 1.4 dynamic-update-slice
  194.7 71.2 %all-reduce = f32[32]{0:T(128)S(1)} all-reduce(f32[32]{0:T(128)S(1)} %dynamic-update-slice), channel_id=1, replica_groups=mesh['dom'=32,'strip'=16] {'dom'}, use_global_device_ids=true, to_apply=%add | all-reduce | flops 32 | bytes 256
  265.8 0.6 reduce_max.9
  266.4 1.3 exponential_reduce_fusion
  269.0 0.6 dynamic_slice.7
  (64 shorter events, 2.4 us)
Async XLA Ops:
  7.2 125.3 %copy-start.2 = (f32[32,512]{1,0:T(8,128)S(1)}, f32[32,512]{1,0:T(8,128)}, u32[]{:S(2)}) copy-start(f32[32,512]{1,0:T(8,128)} %param.8) | copy-start | bytes 196612
  7.2 125.3 %copy-start = (f32[32,512]{1,0:T(8,128)S(1)}, f32[32,512]{1,0:T(8,128)}, u32[]{:S(2)}) copy-start(f32[32,512]{1,0:T(8,128)} %param.9) | copy-start | bytes 196612
  7.2 112.3 %all-gather.2.cloned.1.call-start = ((), (), s32[]{:S(2)}) async-start(), calls=%async_computation | async-start | bytes 8650752 | tf_op jit(solution)/shard_map/all_gather | solution.py:82
  8.7 123.7 %collective-permute-start.2 = (f32[2,8,512]{2,1,0:T(8,128)S(1)}, f32[2,8,512]{2,1,0:T(8,128)S(1)}, u32[]{:S(2)}, u32[]{:S(2)}) collective-permute-start(f32[2,8,512]{2,1,0:T(8,128)S(1)} %get-tuple-element.42), channel_id=1, source_target_pairs={{0,1},{1,2},{2,3},{3,4},{4,5},{5,6},{6,7},{7,8},{8,9},{9,10},{10,1... | collective-permute-start | bytes 98312 | tf_op jit(solution)/shard_map/ppermute | solution.py:21
  10.6 121.8 %collective-permute-start.3 = (f32[2,8,512]{2,1,0:T(8,128)S(1)}, f32[2,8,512]{2,1,0:T(8,128)S(1)}, u32[]{:S(2)}, u32[]{:S(2)}) collective-permute-start(f32[2,8,512]{2,1,0:T(8,128)S(1)} %get-tuple-element.43), channel_id=1, source_target_pairs={{1,0},{2,1},{3,2},{4,3},{5,4},{6,5},{7,6},{8,7},{9,8},{10,9},{11,1... | collective-permute-start | bytes 98312 | tf_op jit(solution)/shard_map/ppermute | solution.py:23
  17.4 132.1 %copy-start.3 = (s32[1,512]{1,0:T(1,128)S(1)}, s32[1,512]{1,0:T(1,128)}, u32[]{:S(2)}) copy-start(s32[1,512]{1,0:T(1,128)} %param.10) | copy-start | bytes 6148
  124.2 7.0 %collective-permute-start = (f32[1,4,2,512]{3,2,1,0:T(2,128)S(1)}, f32[1,4,2,512]{3,2,1,0:T(2,128)S(1)}, u32[]{:S(2)}, u32[]{:S(2)}) collective-permute-start(f32[1,4,2,512]{3,2,1,0:T(2,128)S(1)} %get-tuple-element.32), channel_id=1, source_target_pairs={{0,1},{1,2},{2,3},{3,4},{4,5},{5,6},{6,7},{7,8},{8,9},{9,10},{10,1... | collective-permute-start | bytes 49160 | tf_op jit(solution)/shard_map/ppermute | solution.py:21
  126.1 6.3 %collective-permute-start.1 = (f32[1,4,2,512]{3,2,1,0:T(2,128)S(1)}, f32[1,4,2,512]{3,2,1,0:T(2,128)S(1)}, u32[]{:S(2)}, u32[]{:S(2)}) collective-permute-start(f32[1,4,2,512]{3,2,1,0:T(2,128)S(1)} %get-tuple-element.33), channel_id=1, source_target_pairs={{1,0},{2,1},{3,2},{4,3},{5,4},{6,5},{7,6},{8,7},{9,8},{10,9},{11,1... | collective-permute-start | bytes 49160 | tf_op jit(solution)/shard_map/ppermute | solution.py:23
  133.5 6.8 %collective-permute-start.4 = (f32[1,4,2,512]{3,2,1,0:T(2,128)S(1)}, f32[1,4,2,512]{3,2,1,0:T(2,128)S(1)}, u32[]{:S(2)}, u32[]{:S(2)}) collective-permute-start(f32[1,4,2,512]{3,2,1,0:T(2,128)S(1)} %get-tuple-element.30), channel_id=1, source_target_pairs={{0,1},{1,2},{2,3},{3,4},{4,5},{5,6},{6,7},{7,8},{8,9},{9,10},{10,1... | collective-permute-start | bytes 49160 | tf_op jit(solution)/shard_map/ppermute | solution.py:21
  135.4 6.3 %collective-permute-start.5 = (f32[1,4,2,512]{3,2,1,0:T(2,128)S(1)}, f32[1,4,2,512]{3,2,1,0:T(2,128)S(1)}, u32[]{:S(2)}, u32[]{:S(2)}) collective-permute-start(f32[1,4,2,512]{3,2,1,0:T(2,128)S(1)} %get-tuple-element.31), channel_id=1, source_target_pairs={{1,0},{2,1},{3,2},{4,3},{5,4},{6,5},{7,6},{8,7},{9,8},{10,9},{11,1... | collective-permute-start | bytes 49160 | tf_op jit(solution)/shard_map/ppermute | solution.py:23
  141.8 22.6 %copy-start.4 = (f32[1,512]{1,0:T(1,128)S(1)}, f32[1,512]{1,0:T(1,128)}, u32[]{:S(2)}) copy-start(f32[1,512]{1,0:T(1,128)} %param.11) | copy-start | bytes 6148
  142.7 6.8 %collective-permute-start.6 = (f32[1,4,2,512]{3,2,1,0:T(2,128)S(1)}, f32[1,4,2,512]{3,2,1,0:T(2,128)S(1)}, u32[]{:S(2)}, u32[]{:S(2)}) collective-permute-start(f32[1,4,2,512]{3,2,1,0:T(2,128)S(1)} %get-tuple-element.28), channel_id=1, source_target_pairs={{0,1},{1,2},{2,3},{3,4},{4,5},{5,6},{6,7},{7,8},{8,9},{9,10},{10,1... | collective-permute-start | bytes 49160 | tf_op jit(solution)/shard_map/ppermute | solution.py:21
  144.7 6.3 %collective-permute-start.7 = (f32[1,4,2,512]{3,2,1,0:T(2,128)S(1)}, f32[1,4,2,512]{3,2,1,0:T(2,128)S(1)}, u32[]{:S(2)}, u32[]{:S(2)}) collective-permute-start(f32[1,4,2,512]{3,2,1,0:T(2,128)S(1)} %get-tuple-element.29), channel_id=1, source_target_pairs={{1,0},{2,1},{3,2},{4,3},{5,4},{6,5},{7,6},{8,7},{9,8},{10,9},{11,1... | collective-permute-start | bytes 49160 | tf_op jit(solution)/shard_map/ppermute | solution.py:23
  152.0 8.1 %collective-permute-start.8 = (f32[1,4,2,512]{3,2,1,0:T(2,128)S(1)}, f32[1,4,2,512]{3,2,1,0:T(2,128)S(1)}, u32[]{:S(2)}, u32[]{:S(2)}) collective-permute-start(f32[1,4,2,512]{3,2,1,0:T(2,128)S(1)} %get-tuple-element.26), channel_id=1, source_target_pairs={{0,1},{1,2},{2,3},{3,4},{4,5},{5,6},{6,7},{7,8},{8,9},{9,10},{10,1... | collective-permute-start | bytes 49160 | tf_op jit(solution)/shard_map/ppermute | solution.py:21
  153.9 6.3 %collective-permute-start.9 = (f32[1,4,2,512]{3,2,1,0:T(2,128)S(1)}, f32[1,4,2,512]{3,2,1,0:T(2,128)S(1)}, u32[]{:S(2)}, u32[]{:S(2)}) collective-permute-start(f32[1,4,2,512]{3,2,1,0:T(2,128)S(1)} %get-tuple-element.27), channel_id=1, source_target_pairs={{1,0},{2,1},{3,2},{4,3},{5,4},{6,5},{7,6},{8,7},{9,8},{10,9},{11,1... | collective-permute-start | bytes 49160 | tf_op jit(solution)/shard_map/ppermute | solution.py:23
  161.2 108.4 %copy-start.1 = (f32[1,4,32,512]{3,2,1,0:T(8,128)}, f32[1,4,32,512]{3,2,1,0:T(8,128)S(1)}, u32[]{:S(2)}) copy-start(f32[1,4,32,512]{3,2,1,0:T(8,128)S(1)} %maximum_select_fusion.3) | copy-start | bytes 786436
Sparse Core Ops, SparseCore 0:
  11.2 108.3 all-gather.1
where the time goes:
time: 277 us; the launch traced here: 276 us
  waiting for transfers between devices  107 us (39%)
  blocking collectives  98.8 us (36%)
  starting transfers between devices  33.9 us (12%)
  between operations  16.5 us (6%)
  other arithmetic  10.4 us (4%)
  local copies, waits for them, and re-layouts  9.92 us (4%)
    all_gather x1, waiting for transfers between devices, local(): piece = lax.all_gather(state, 'dom', axis=0, tiled=True)  102 us
    unnamed x1, blocking collectives  71.2 us
    psum x1, blocking collectives, local(): summed = lax.psum(partial_value, 'strip')  27.6 us
    ppermute x5, starting transfers between devices, padded_2(): lax.ppermute(head, axis, [((i + 1) % count, i) for i in range(ends)])  24.3 us
    ppermute x5, starting transfers between devices, padded_2(): lax.ppermute(tail, axis, [(i, (i + 1) % count) for i in range(ends)])  9.59 us
  transfers between devices with their start and end apart: 11, of which 5 were waited for; matrix products, arithmetic and copies ran while one was open for 3% of the time, Pallas kernels for 0%

commit v1 on v0

--- a/solution.py
+++ b/solution.py
@@ -103,7 +103,9 @@
     seen = jnp.take(eta, obs_cells[0], axis=1)
     gap = seen - obs_values[0][None, :]
     partial_value = -jnp.sum(gap * gap, axis=1) * (0.5 / obs_variance)
-    summed = lax.psum(partial_value, "strip")
+    summed = partial_value
+    for hop in (1, 2, 4, 8):
+        summed = summed + lax.ppermute(summed, "strip", [(dev, dev ^ hop) for dev in range(16)])
     loglik = lax.all_gather(summed, "dom", axis=0, tiled=True)
     top = jnp.max(loglik)
     total = top + jnp.log(jnp.sum(jnp.exp(loglik - top)))

time: 277 us -> 278 us (level)
  the two profiles are of different devices: /device:TPU:32 before, /device:TPU:24 now
where the time goes in v1:
time: 278 us
  waiting for transfers between devices  121 us (44%)
  blocking collectives  71.2 us (26%)
  starting transfers between devices  47.5 us (17%)
  between operations  18.3 us (7%)
  other arithmetic  11.7 us (4%)
  local copies, waits for them, and re-layouts  8.5 us (3%)
    all_gather x1, waiting for transfers between devices, local(): piece = lax.all_gather(state, 'dom', axis=0, tiled=True)  103 us
    unnamed x1, blocking collectives  71.2 us
    ppermute x5, starting transfers between devices, padded_2(): lax.ppermute(tail, axis, [(i, (i + 1) % count) for i in range(ends)])  19.1 us
    ppermute x4, starting transfers between devices, local(): lax.ppermute(summed, 'strip', [(dev, dev ^ hop) for dev in range(16)])  15.3 us
    ppermute x5, starting transfers between devices, padded_2(): lax.ppermute(head, axis, [((i + 1) % count, i) for i in range(ends)])  13 us
    ppermute x4, waiting for transfers between devices, local(): lax.ppermute(summed, 'strip', [(dev, dev ^ hop) for dev in range(16)])  11.9 us
  transfers between devices with their start and end apart: 15, of which 8 were waited for; matrix products, arithmetic and copies ran while one was open for 3% of the time, Pallas kernels for 0%

profile of v1, /device:TPU:24, one launch (start us, length us, event | category | flops | bytes accessed | tf_op | source)
XLA Modules:
  0.0 277.6 jit_solution(12657075726423839680)
XLA Ops:
  7.2 0.7 all-gather.2.cloned.1.call-update
  7.9 0.8 pad_maximum_fusion.24
  8.7 1.9 collective-permute-start.2
  10.6 3.6 %collective-permute-start.3 = (f32[2,8,512]{2,1,0:T(8,128)S(1)}, f32[2,8,512]{2,1,0:T(8,128)S(1)}, u32[]{:S(2)}, u32[]{:S(2)}) collective-permute-start(f32[2,8,512]{2,1,0:T(8,128)S(1)} %get-tuple-element.43), channel_id=1, source_target_pairs={{1,0},{2,1},{3,2},{4,3},{5,4},{6,5},{7,6},{8,7},{9,8},{10,9},{11,1... | collective-permute-start | bytes 98312 | tf_op jit(solution)/shard_map/ppermute | solution.py:23
  14.3 1.2 dynamic_slice.6
  15.5 0.6 iota_compare_fusion
  16.2 103.4 %all-gather.2.cloned.1.call-done = f32[32,4,32,512]{3,2,1,0:T(8,128)} async-done(((f32[1,4,32,512]{3,2,1,0:T(8,128)}), f32[32,4,32,512]{3,2,1,0:T(8,128)}) %all-gather.2.cloned.1.call-update) | async-done | bytes 8388624 | tf_op jit(solution)/shard_map/all_gather | solution.py:82
  119.6 4.6 %select_reduce_fusion = f32[4,32,512]{2,1,0:T(8,128)S(1)} fusion(f32[32,4,32,512]{3,2,1,0:T(8,128)} %all-gather.2.cloned.1.call-done, pred[32]{0:T(512)(128)(4,1)S(1)} %iota_compare_fusion), kind=kLoop, calls=%fused_computation.1 | loop fusion | flops 4128768 | bytes 8650784 | tf_op jit(solution)/shard_map/reduce_sum | solution.py:85
  124.2 1.9 collective-permute-start
  126.2 3.6 %collective-permute-start.1 = (f32[1,4,2,512]{3,2,1,0:T(2,128)S(1)}, f32[1,4,2,512]{3,2,1,0:T(2,128)S(1)}, u32[]{:S(2)}, u32[]{:S(2)}) collective-permute-start(f32[1,4,2,512]{3,2,1,0:T(2,128)S(1)} %get-tuple-element.33), channel_id=1, source_target_pairs={{1,0},{2,1},{3,2},{4,3},{5,4},{6,5},{7,6},{8,7},{9,8},{10,9},{11,1... | collective-permute-start | bytes 49160 | tf_op jit(solution)/shard_map/ppermute | solution.py:23
  130.0 1.6 collective-permute-done.1
  131.9 0.1 fusion.25
  132.3 0.1 fusion.52
  132.4 0.1 add_bitcast_fusion.3
  132.5 0.1 maximum_select_fusion
  132.7 5.6 %collective-permute-start.4 = (f32[1,4,2,512]{3,2,1,0:T(2,128)S(1)}, f32[1,4,2,512]{3,2,1,0:T(2,128)S(1)}, u32[]{:S(2)}, u32[]{:S(2)}) collective-permute-start(f32[1,4,2,512]{3,2,1,0:T(2,128)S(1)} %get-tuple-element.30), channel_id=1, source_target_pairs={{0,1},{1,2},{2,3},{3,4},{4,5},{5,6},{6,7},{7,8},{8,9},{9,10},{10,1... | collective-permute-start | bytes 49160 | tf_op jit(solution)/shard_map/ppermute | solution.py:21
  138.3 1.9 collective-permute-start.5
  140.2 1.4 collective-permute-done.5
  141.9 0.1 fusion.18
  142.3 0.1 fusion.57
  142.4 0.1 add_bitcast_fusion.2
  142.7 4.9 %collective-permute-start.6 = (f32[1,4,2,512]{3,2,1,0:T(2,128)S(1)}, f32[1,4,2,512]{3,2,1,0:T(2,128)S(1)}, u32[]{:S(2)}, u32[]{:S(2)}) collective-permute-start(f32[1,4,2,512]{3,2,1,0:T(2,128)S(1)} %get-tuple-element.28), channel_id=1, source_target_pairs={{0,1},{1,2},{2,3},{3,4},{4,5},{5,6},{6,7},{7,8},{8,9},{9,10},{10,1... | collective-permute-start | bytes 49160 | tf_op jit(solution)/shard_map/ppermute | solution.py:21
  147.5 1.9 collective-permute-start.7
  149.5 1.4 collective-permute-done.7
  151.1 0.1 fusion.11
  151.6 0.1 fusion.62
  151.7 0.1 add_bitcast_fusion.1
  151.9 4.9 %collective-permute-start.8 = (f32[1,4,2,512]{3,2,1,0:T(2,128)S(1)}, f32[1,4,2,512]{3,2,1,0:T(2,128)S(1)}, u32[]{:S(2)}, u32[]{:S(2)}) collective-permute-start(f32[1,4,2,512]{3,2,1,0:T(2,128)S(1)} %get-tuple-element.26), channel_id=1, source_target_pairs={{0,1},{1,2},{2,3},{3,4},{4,5},{5,6},{6,7},{7,8},{8,9},{9,10},{10,1... | collective-permute-start | bytes 49160 | tf_op jit(solution)/shard_map/ppermute | solution.py:21
  156.8 1.9 collective-permute-start.9
  158.7 1.3 dynamic-slice
  160.0 0.1 collective-permute-done.9
  160.4 0.1 fusion.4
  160.8 0.1 fusion.67
  160.9 0.1 add_bitcast_fusion
  161.2 3.1 %gather_fusion = f32[512]{0:T(512)S(1)} fusion(f32[16384]{0:T(1024)S(1)} %bitcast.118, s32[1024]{0:T(1024)S(1)} %pad_clamp_fusion), kind=kCustom, calls=%fused_computation | custom fusion | bytes 6144 | tf_op jit(solution)/shard_map/jit(_take)/gather | solution.py:103
  164.3 0.6 multiply_reduce_fusion
  165.5 5.7 %collective-permute-start.10 = (f32[1]{0:T(128)}, f32[1]{0:T(128)}, u32[]{:S(2)}, u32[]{:S(2)}) collective-permute-start(f32[1]{0:T(128)} %bitcast.40), channel_id=1, source_target_pairs={{0,1},{1,0},{2,3},{3,2},{4,5},{5,4},{6,7},{7,6},{8,9},{9,8},{10,11... | collective-permute-start | bytes 20 | tf_op jit(solution)/shard_map/ppermute | solution.py:108
  171.8 3.2 %collective-permute-start.11 = (f32[1]{0:T(128)}, f32[1]{0:T(128)}, u32[]{:S(2)}, u32[]{:S(2)}) collective-permute-start(f32[1]{0:T(128)} %add.167), channel_id=1, source_target_pairs={{0,2},{1,3},{2,0},{3,1},{4,6},{5,7},{6,4},{7,5},{8,10},{9,11},{10,... | collective-permute-start | bytes 20 | tf_op jit(solution)/shard_map/ppermute | solution.py:108
  175.0 2.4 collective-permute-done.11
  178.0 3.2 %collective-permute-start.12 = (f32[1]{0:T(128)}, f32[1]{0:T(128)}, u32[]{:S(2)}, u32[]{:S(2)}) collective-permute-start(f32[1]{0:T(128)} %add.168), channel_id=1, source_target_pairs={{0,4},{1,5},{2,6},{3,7},{4,0},{5,1},{6,2},{7,3},{8,12},{9,13},{10,... | collective-permute-start | bytes 20 | tf_op jit(solution)/shard_map/ppermute | solution.py:108
  181.2 3.3 %collective-permute-done.12 = f32[1]{0:T(128)} collective-permute-done((f32[1]{0:T(128)}, f32[1]{0:T(128)}, u32[]{:S(2)}, u32[]{:S(2)}) %collective-permute-start.12) | collective-permute-done | bytes 36 | tf_op jit(solution)/shard_map/ppermute | solution.py:108
  185.1 3.2 %collective-permute-start.13 = (f32[1]{0:T(128)}, f32[1]{0:T(128)}, u32[]{:S(2)}, u32[]{:S(2)}) collective-permute-start(f32[1]{0:T(128)} %add.169), channel_id=1, source_target_pairs={{0,8},{1,9},{2,10},{3,11},{4,12},{5,13},{6,14},{7,15},{8,0},{9,1},... | collective-permute-start | bytes 20 | tf_op jit(solution)/shard_map/ppermute | solution.py:108
  188.3 6.3 %collective-permute-done.13 = f32[1]{0:T(128)} collective-permute-done((f32[1]{0:T(128)}, f32[1]{0:T(128)}, u32[]{:S(2)}, u32[]{:S(2)}) %collective-permute-start.13) | collective-permute-done | bytes 36 | tf_op jit(solution)/shard_map/ppermute | solution.py:108
  194.6 1.4 add_dynamic-update-slice_fusion
  195.9 71.2 %all-reduce = f32[32]{0:T(128)S(1)} all-reduce(f32[32]{0:T(128)S(1)} %add_dynamic-update-slice_fusion), channel_id=1, replica_groups=mesh['dom'=32,'strip'=16] {'dom'}, use_global_device_ids=true, to_apply=%add | all-reduce | flops 32 | bytes 256
  267.1 0.6 reduce_max.9
  267.7 1.2 exponential_reduce_fusion
  270.2 0.6 dynamic_slice.7
  (71 shorter events, 2.9 us)
Async XLA Ops:
  7.2 124.5 %copy-start.2 = (f32[32,512]{1,0:T(8,128)S(1)}, f32[32,512]{1,0:T(8,128)}, u32[]{:S(2)}) copy-start(f32[32,512]{1,0:T(8,128)} %param.8) | copy-start | bytes 196612
  7.2 124.5 %copy-start = (f32[32,512]{1,0:T(8,128)S(1)}, f32[32,512]{1,0:T(8,128)}, u32[]{:S(2)}) copy-start(f32[32,512]{1,0:T(8,128)} %param.9) | copy-start | bytes 196612
  7.2 112.4 %all-gather.2.cloned.1.call-start = ((), (), s32[]{:S(2)}) async-start(), calls=%async_computation | async-start | bytes 8650752 | tf_op jit(solution)/shard_map/all_gather | solution.py:82
  8.7 122.9 %collective-permute-start.2 = (f32[2,8,512]{2,1,0:T(8,128)S(1)}, f32[2,8,512]{2,1,0:T(8,128)S(1)}, u32[]{:S(2)}, u32[]{:S(2)}) collective-permute-start(f32[2,8,512]{2,1,0:T(8,128)S(1)} %get-tuple-element.42), channel_id=1, source_target_pairs={{0,1},{1,2},{2,3},{3,4},{4,5},{5,6},{6,7},{7,8},{8,9},{9,10},{10,1... | collective-permute-start | bytes 98312 | tf_op jit(solution)/shard_map/ppermute | solution.py:21
  10.6 121.0 %collective-permute-start.3 = (f32[2,8,512]{2,1,0:T(8,128)S(1)}, f32[2,8,512]{2,1,0:T(8,128)S(1)}, u32[]{:S(2)}, u32[]{:S(2)}) collective-permute-start(f32[2,8,512]{2,1,0:T(8,128)S(1)} %get-tuple-element.43), channel_id=1, source_target_pairs={{1,0},{2,1},{3,2},{4,3},{5,4},{6,5},{7,6},{8,7},{9,8},{10,9},{11,1... | collective-permute-start | bytes 98312 | tf_op jit(solution)/shard_map/ppermute | solution.py:23
  16.2 133.3 %copy-start.3 = (s32[1,512]{1,0:T(1,128)S(1)}, s32[1,512]{1,0:T(1,128)}, u32[]{:S(2)}) copy-start(s32[1,512]{1,0:T(1,128)} %param.10) | copy-start | bytes 6148
  124.2 5.7 %collective-permute-start = (f32[1,4,2,512]{3,2,1,0:T(2,128)S(1)}, f32[1,4,2,512]{3,2,1,0:T(2,128)S(1)}, u32[]{:S(2)}, u32[]{:S(2)}) collective-permute-start(f32[1,4,2,512]{3,2,1,0:T(2,128)S(1)} %get-tuple-element.32), channel_id=1, source_target_pairs={{0,1},{1,2},{2,3},{3,4},{4,5},{5,6},{6,7},{7,8},{8,9},{9,10},{10,1... | collective-permute-start | bytes 49160 | tf_op jit(solution)/shard_map/ppermute | solution.py:21
  126.2 5.4 %collective-permute-start.1 = (f32[1,4,2,512]{3,2,1,0:T(2,128)S(1)}, f32[1,4,2,512]{3,2,1,0:T(2,128)S(1)}, u32[]{:S(2)}, u32[]{:S(2)}) collective-permute-start(f32[1,4,2,512]{3,2,1,0:T(2,128)S(1)} %get-tuple-element.33), channel_id=1, source_target_pairs={{1,0},{2,1},{3,2},{4,3},{5,4},{6,5},{7,6},{8,7},{9,8},{10,9},{11,1... | collective-permute-start | bytes 49160 | tf_op jit(solution)/shard_map/ppermute | solution.py:23
  132.7 7.5 %collective-permute-start.4 = (f32[1,4,2,512]{3,2,1,0:T(2,128)S(1)}, f32[1,4,2,512]{3,2,1,0:T(2,128)S(1)}, u32[]{:S(2)}, u32[]{:S(2)}) collective-permute-start(f32[1,4,2,512]{3,2,1,0:T(2,128)S(1)} %get-tuple-element.30), channel_id=1, source_target_pairs={{0,1},{1,2},{2,3},{3,4},{4,5},{5,6},{6,7},{7,8},{8,9},{9,10},{10,1... | collective-permute-start | bytes 49160 | tf_op jit(solution)/shard_map/ppermute | solution.py:21
  138.3 3.4 %collective-permute-start.5 = (f32[1,4,2,512]{3,2,1,0:T(2,128)S(1)}, f32[1,4,2,512]{3,2,1,0:T(2,128)S(1)}, u32[]{:S(2)}, u32[]{:S(2)}) collective-permute-start(f32[1,4,2,512]{3,2,1,0:T(2,128)S(1)} %get-tuple-element.31), channel_id=1, source_target_pairs={{1,0},{2,1},{3,2},{4,3},{5,4},{6,5},{7,6},{8,7},{9,8},{10,9},{11,1... | collective-permute-start | bytes 49160 | tf_op jit(solution)/shard_map/ppermute | solution.py:23
  141.8 22.6 %copy-start.4 = (f32[1,512]{1,0:T(1,128)S(1)}, f32[1,512]{1,0:T(1,128)}, u32[]{:S(2)}) copy-start(f32[1,512]{1,0:T(1,128)} %param.11) | copy-start | bytes 6148
  142.7 6.8 %collective-permute-start.6 = (f32[1,4,2,512]{3,2,1,0:T(2,128)S(1)}, f32[1,4,2,512]{3,2,1,0:T(2,128)S(1)}, u32[]{:S(2)}, u32[]{:S(2)}) collective-permute-start(f32[1,4,2,512]{3,2,1,0:T(2,128)S(1)} %get-tuple-element.28), channel_id=1, source_target_pairs={{0,1},{1,2},{2,3},{3,4},{4,5},{5,6},{6,7},{7,8},{8,9},{9,10},{10,1... | collective-permute-start | bytes 49160 | tf_op jit(solution)/shard_map/ppermute | solution.py:21
  147.5 3.4 %collective-permute-start.7 = (f32[1,4,2,512]{3,2,1,0:T(2,128)S(1)}, f32[1,4,2,512]{3,2,1,0:T(2,128)S(1)}, u32[]{:S(2)}, u32[]{:S(2)}) collective-permute-start(f32[1,4,2,512]{3,2,1,0:T(2,128)S(1)} %get-tuple-element.29), channel_id=1, source_target_pairs={{1,0},{2,1},{3,2},{4,3},{5,4},{6,5},{7,6},{8,7},{9,8},{10,9},{11,1... | collective-permute-start | bytes 49160 | tf_op jit(solution)/shard_map/ppermute | solution.py:23
  151.9 8.1 %collective-permute-start.8 = (f32[1,4,2,512]{3,2,1,0:T(2,128)S(1)}, f32[1,4,2,512]{3,2,1,0:T(2,128)S(1)}, u32[]{:S(2)}, u32[]{:S(2)}) collective-permute-start(f32[1,4,2,512]{3,2,1,0:T(2,128)S(1)} %get-tuple-element.26), channel_id=1, source_target_pairs={{0,1},{1,2},{2,3},{3,4},{4,5},{5,6},{6,7},{7,8},{8,9},{9,10},{10,1... | collective-permute-start | bytes 49160 | tf_op jit(solution)/shard_map/ppermute | solution.py:21
  156.8 3.4 %collective-permute-start.9 = (f32[1,4,2,512]{3,2,1,0:T(2,128)S(1)}, f32[1,4,2,512]{3,2,1,0:T(2,128)S(1)}, u32[]{:S(2)}, u32[]{:S(2)}) collective-permute-start(f32[1,4,2,512]{3,2,1,0:T(2,128)S(1)} %get-tuple-element.27), channel_id=1, source_target_pairs={{1,0},{2,1},{3,2},{4,3},{5,4},{6,5},{7,6},{8,7},{9,8},{10,9},{11,1... | collective-permute-start | bytes 49160 | tf_op jit(solution)/shard_map/ppermute | solution.py:23
  161.1 109.7 %copy-start.1 = (f32[1,4,32,512]{3,2,1,0:T(8,128)}, f32[1,4,32,512]{3,2,1,0:T(8,128)S(1)}, u32[]{:S(2)}) copy-start(f32[1,4,32,512]{3,2,1,0:T(8,128)S(1)} %maximum_select_fusion.3) | copy-start | bytes 786436
  165.5 5.7 %collective-permute-start.10 = (f32[1]{0:T(128)}, f32[1]{0:T(128)}, u32[]{:S(2)}, u32[]{:S(2)}) collective-permute-start(f32[1]{0:T(128)} %bitcast.40), channel_id=1, source_target_pairs={{0,1},{1,0},{2,3},{3,2},{4,5},{5,4},{6,7},{7,6},{8,9},{9,8},{10,11... | collective-permute-start | bytes 20 | tf_op jit(solution)/shard_map/ppermute | solution.py:108
  171.8 5.6 %collective-permute-start.11 = (f32[1]{0:T(128)}, f32[1]{0:T(128)}, u32[]{:S(2)}, u32[]{:S(2)}) collective-permute-start(f32[1]{0:T(128)} %add.167), channel_id=1, source_target_pairs={{0,2},{1,3},{2,0},{3,1},{4,6},{5,7},{6,4},{7,5},{8,10},{9,11},{10,... | collective-permute-start | bytes 20 | tf_op jit(solution)/shard_map/ppermute | solution.py:108
  178.0 6.5 %collective-permute-start.12 = (f32[1]{0:T(128)}, f32[1]{0:T(128)}, u32[]{:S(2)}, u32[]{:S(2)}) collective-permute-start(f32[1]{0:T(128)} %add.168), channel_id=1, source_target_pairs={{0,4},{1,5},{2,6},{3,7},{4,0},{5,1},{6,2},{7,3},{8,12},{9,13},{10,... | collective-permute-start | bytes 20 | tf_op jit(solution)/shard_map/ppermute | solution.py:108
  185.1 9.5 %collective-permute-start.13 = (f32[1]{0:T(128)}, f32[1]{0:T(128)}, u32[]{:S(2)}, u32[]{:S(2)}) collective-permute-start(f32[1]{0:T(128)} %add.169), channel_id=1, source_target_pairs={{0,8},{1,9},{2,10},{3,11},{4,12},{5,13},{6,14},{7,15},{8,0},{9,1},... | collective-permute-start | bytes 20 | tf_op jit(solution)/shard_map/ppermute | solution.py:108
Sparse Core Ops, SparseCore 0:
  11.2 108.4 all-gather.1
